TPU v7x, 32 devices: a whole 2x2x4 slice. The times are simulated.
32 devices in a mesh: grp: 2 (over x), section: 16 (over z, y, core).
Axes of the slice: x: 2, y: 2, z: 4, core: 2. Of those that a mesh axis runs over, the one named last changes fastest.
Arguments:
- latent: bfloat16 [1536, 64], P(('grp', 'section')), parts along dimension 0, may hold values from -6 to 6
- control_latent: bfloat16 [1536, 64], P(('grp', 'section')), parts along dimension 0, may hold values from -6 to 6
- patch_tiles: int32 [4], replicated, may hold values from 1 to 2, 6 in all
- tile_lists: int32 [2, 6, 3], replicated, may hold values from 0 to 5, as said below
- tile_counts: int32 [2, 6], replicated, may hold values from 1 to 3, as said below
- embed_weight: bfloat16 [64, 3072], replicated, may hold values from -0.75 to 0.75
- control_embed: bfloat16 [64, 3072], replicated, may hold values from -0.75 to 0.75
- modulation: float32 [2, 3, 3072], replicated, may hold values from -4 to 4
- qk_gain: float32 [2, 2, 128], replicated, may hold values from 0.1 to 1.9
- qkv_weight: bfloat16 [16, 3072, 1152], P('section'), may hold values from -0.109375 to 0.109375
- out_weight: bfloat16 [16, 384, 3072], P('section'), may hold values from -0.109375 to 0.109375
- stale_cache: bfloat16 [16, 1536, 768], P('section', 'grp'), parts along dimension 1, may hold values from -6 to 6
- control_gain: float32 [1, 3072], replicated, may hold values from -3 to 3
- final_mod: float32 [2, 3072], replicated, may hold values from -3 to 3
- final_weight: bfloat16 [3072, 64], replicated, may hold values from -0.109375 to 0.109375
Outputs:
- denoised: float32 [1536, 64], P(('grp', 'section')), parts along dimension 0
There are 2 independent parts, one for each index of `grp`. A program takes and returns all parts, laid end to end along the dimension named above; an argument that names none is the same for every part. Nothing has to cross between parts.
Inputs may be any that keep to these rules, and one draw needn't show every extreme that they name: `patch_tiles`: the patches are contiguous and in order and together cover all 6 tiles; the largest has exactly 2 tiles. Entry 0 of tile_lists[b, t] is t itself; the 3 entries of one row are distinct. `tile_counts`: in every block slot some query tile uses all 3 listed tiles.
All inputs are finite; a program needn't handle non-finite values.
Results may differ from a plain program's by a relative error of at most 0.014.
Values may be sent and summed in bfloat16 or wider, within the bound.
No kernel may reach another device: no remote copies, remote signals or barrier semaphores. Data moves between devices by JAX's collectives and lax.ppermute only.
A program may use at most 64 MiB of HBM per device.

v0:
```python
import math
import jax
import jax.numpy as jnp
from jax import lax
from jax.sharding import PartitionSpec as P

D = 3072
HD = 128
HG = 8
C_OUT = 64
TILE = 128
KSEL = 3
PATCHES = 4
TILES = 6
PMAX = 2
EPSILON = 1e-06


def from_partner(value, axis, distance):
    return lax.ppermute(value, axis, [(i, i ^ 1 << distance) for i in range(lax.axis_size(axis))])


def from_behind(value, axis, steps):
    count = lax.axis_size(axis)
    leading, last = (max(0, -steps), min(count, count - steps))
    return lax.ppermute(value, axis, [(source, source + steps) for source in range(leading, last)])


def modulated(hidden, shift_row, scale_row):
    values = hidden.astype(jnp.float32)
    centered = values - jnp.mean(values, axis=-1, keepdims=True)
    variance = jnp.mean(centered * centered, axis=-1, keepdims=True)
    normed = centered * lax.rsqrt(variance + EPSILON)
    return (normed * (1.0 + scale_row) + shift_row).astype(jnp.bfloat16)


def rms_scaled(values, gain_row):
    return (
        values * lax.rsqrt(jnp.mean(values * values, axis=-1, keepdims=True) + EPSILON) * gain_row
    )


def attend_group(
    modded, w_qkv, w_out, memory, gain_pair, start_tile, patch_length, tile_list, tile_limit
):
    row_count = modded.shape[0]
    query_tiles_count = row_count // TILE
    head_count = w_out.shape[0] // HD
    projected = jnp.dot(modded, w_qkv, preferred_element_type=jnp.float32).reshape(
        row_count, 3, head_count, HD
    )
    queries = rms_scaled(projected[:, 0], gain_pair[0]).astype(jnp.bfloat16)
    keys_new = rms_scaled(projected[:, 1], gain_pair[1]).astype(jnp.bfloat16)
    values_new = projected[:, 2].astype(jnp.bfloat16)
    fresh_rows = jnp.concatenate(
        [
            keys_new.reshape(row_count, head_count * HD),
            values_new.reshape(row_count, head_count * HD),
        ],
        axis=1,
    )
    row_start = start_tile * TILE
    previous = lax.dynamic_slice_in_dim(memory, row_start, row_count, 0)
    live_rows = jnp.arange(row_count) < patch_length * TILE
    memory = lax.dynamic_update_slice_in_dim(
        memory, jnp.where(live_rows[:, None], fresh_rows, previous), row_start, 0
    )
    tiled_memory = memory.reshape(-1, TILE, 2, head_count, HD)
    query_tiles = jnp.minimum(start_tile + jnp.arange(query_tiles_count), TILES - 1)
    picked = tile_list[query_tiles]
    used_counts = tile_limit[query_tiles]
    chosen = tiled_memory[picked]
    key_rows = chosen[:, :, :, 0].reshape(query_tiles_count, KSEL * TILE, head_count, HD)
    value_rows = chosen[:, :, :, 1].reshape(query_tiles_count, KSEL * TILE, head_count, HD)
    query_rows = queries.reshape(query_tiles_count, TILE, head_count, HD)
    scores = jnp.einsum(
        "tqhd,tkhd->thqk", query_rows, key_rows, preferred_element_type=jnp.float32
    ) / math.sqrt(HD)
    allowed = (jnp.arange(KSEL * TILE) // TILE)[None, :] < used_counts[:, None]
    scores = jnp.where(allowed[:, None, None, :], scores, -1e30)
    highest = jnp.max(scores, axis=-1, keepdims=True)
    weights = jnp.exp(scores - highest)
    probabilities = (weights / jnp.sum(weights, axis=-1, keepdims=True)).astype(jnp.bfloat16)
    attended = jnp.einsum(
        "thqk,tkhd->tqhd", probabilities, value_rows, preferred_element_type=jnp.float32
    ).astype(jnp.bfloat16)
    attended = attended.reshape(row_count, head_count * HD)
    partial_value = jnp.dot(attended, w_out, preferred_element_type=jnp.float32)
    return (partial_value, memory)


def split_rows(current, upper_half):
    middle = current.shape[0] // 2
    kept = jnp.where(upper_half, current[middle:], current[:middle])
    given = jnp.where(upper_half, current[:middle], current[middle:])
    return (kept, given)


def on_device(
    latent,
    control_latent,
    patch_tiles,
    tile_lists,
    tile_counts,
    embed_weight,
    control_embed,
    modulation,
    qk_gain,
    qkv_weight,
    out_weight,
    stale_cache,
    control_gain,
    final_mod,
    final_weight,
):
    slot_count = lax.axis_size("section") // HG
    control_count = slot_count // 2
    device_index = lax.axis_index("section")
    slot_index = device_index // HG
    group_index = device_index % HG
    is_control = slot_index % 2 == 0
    chain_index = slot_index // 2
    row_count = PMAX * TILE
    share_rows = row_count // HG
    bit_count = HG.bit_length() - 1
    bit_order = list(range(bit_count - 1, -1, -1))
    share_start = jnp.zeros((), jnp.int32)
    for position, bit_index in enumerate(bit_order):
        share_start = share_start + (group_index >> bit_index & 1) * (row_count >> position + 1)
    whole_latent, whole_control = (
        lax.all_gather(latent, "section", axis=0, tiled=True),
        lax.all_gather(control_latent, "section", axis=0, tiled=True),
    )
    padding = ((0, row_count), (0, 0))
    latent_pad = jnp.pad(whole_latent, padding)
    control_pad = jnp.pad(whole_control, padding)
    seq_rows = whole_latent.shape[0]
    memory_start = jnp.pad(stale_cache[0], padding)
    w_qkv = qkv_weight[0]
    w_out = out_weight[0]
    shifts = modulation[slot_index]
    gain_pair = qk_gain[slot_index]
    tile_list = tile_lists[slot_index]
    tile_limit = tile_counts[slot_index]
    control_row = control_gain[jnp.minimum(chain_index, control_count - 1)]
    is_last_main = slot_index == slot_count - 1
    starts = jnp.cumsum(patch_tiles) - patch_tiles

    def reduce_share(partial_value):
        upper_half = group_index >> bit_order[0] & 1 == 1
        kept, given = split_rows(partial_value.astype(jnp.bfloat16), upper_half)
        summed = kept.astype(jnp.float32) + from_partner(given, "section", bit_order[0]).astype(
            jnp.float32
        )
        for bit_index in bit_order[1:]:
            upper_half = group_index >> bit_index & 1 == 1
            kept, given = split_rows(summed, upper_half)
            summed = kept + from_partner(given.astype(jnp.bfloat16), "section", bit_index).astype(
                given.dtype
            )
        return summed

    def gather_rows(gathered):
        for bit_index in reversed(bit_order):
            partner = from_partner(gathered, "section", bit_index)
            upper_half = group_index >> bit_index & 1 == 1
            gathered = jnp.where(
                upper_half,
                jnp.concatenate([partner, gathered]),
                jnp.concatenate([gathered, partner]),
            )
        return gathered

    def run_tick(tick_index, carry):
        inflow_hidden, inflow_control, memory, denoised = carry
        patch_index = tick_index - slot_index
        active = (patch_index >= 0) & (patch_index < PATCHES)
        patch_index = jnp.clip(patch_index, 0, PATCHES - 1)
        start_tile = starts[patch_index]
        patch_length = patch_tiles[patch_index]
        row_start = start_tile * TILE + share_start
        own_latent = lax.dynamic_slice_in_dim(latent_pad, row_start, share_rows, 0)
        own_control = lax.dynamic_slice_in_dim(control_pad, row_start, share_rows, 0)
        embedded = jnp.dot(own_latent, embed_weight, preferred_element_type=jnp.float32)
        conditioned = embedded + jnp.dot(
            own_control, control_embed, preferred_element_type=jnp.float32
        )
        first_slot = slot_index == 0
        current_hidden = jnp.where(first_slot, embedded.astype(jnp.bfloat16), inflow_hidden)
        current_control = jnp.where(first_slot, conditioned.astype(jnp.bfloat16), inflow_control)
        stream = jnp.where(is_control, current_control, current_hidden)
        gathered = gather_rows(stream)

        def compute(memory_in):
            modded = modulated(gathered, shifts[0], shifts[1])
            return attend_group(
                modded,
                w_qkv,
                w_out,
                memory_in,
                gain_pair,
                start_tile,
                patch_length,
                tile_list,
                tile_limit,
            )

        def skipped(memory_in):
            return (jnp.zeros((row_count, w_out.shape[1]), jnp.float32), memory_in)

        partial_value, memory = lax.cond(active, compute, skipped, memory)
        summed = reduce_share(partial_value)
        updated = stream.astype(jnp.float32) + shifts[2] * summed
        new_control = updated.astype(jnp.bfloat16)
        new_hidden = (updated + control_row * current_control.astype(jnp.float32)).astype(
            jnp.bfloat16
        )
        out_hidden = jnp.where(is_control, current_hidden, new_hidden)
        out_control = jnp.where(is_control, new_control, current_control)
        final_rows = jnp.dot(
            modulated(out_hidden, final_mod[0], final_mod[1]),
            final_weight,
            preferred_element_type=jnp.float32,
        )
        live_rows = (
            active & is_last_main & (share_start + jnp.arange(share_rows) < patch_length * TILE)
        )
        previous = lax.dynamic_slice_in_dim(denoised, row_start, share_rows, 0)
        denoised = lax.dynamic_update_slice_in_dim(
            denoised, jnp.where(live_rows[:, None], final_rows, previous), row_start, 0
        )
        inflow_hidden, inflow_control = from_behind((out_hidden, out_control), "section", HG)
        return (inflow_hidden, inflow_control, memory, denoised)

    empty_share = jnp.zeros((share_rows, D), jnp.bfloat16)
    initial = (
        empty_share,
        empty_share,
        memory_start,
        jnp.zeros((seq_rows + row_count, C_OUT), jnp.float32),
    )
    finished = lax.fori_loop(0, slot_count + PATCHES - 1, run_tick, initial)
    return lax.psum_scatter(finished[3][:seq_rows], "section", scatter_dimension=0, tiled=True)


def solution(mesh):
    return jax.shard_map(
        on_device,
        mesh=mesh,
        in_specs=(
            P(("grp", "section"), None),
            P(("grp", "section"), None),
            P(),
            P(),
            P(),
            P(),
            P(),
            P(),
            P(),
            P("section", None, None),
            P("section", None, None),
            P("section", "grp", None),
            P(),
            P(),
            P(),
        ),
        out_specs=P(("grp", "section"), None),
        check_vma=False,
    )
```

profile of v0, /device:TPU:0, one launch (start us, length us, event | category | flops | bytes accessed | tf_op | source)
XLA Modules:
  0.0 692.2 jit_solution(14145736935525604301)
XLA Ops:
  8.5 23.6 %all_gather.6 = bf16[768,64]{1,0:T(8,128)(2,1)S(1)} all-gather(bf16[48,64]{1,0:T(8,128)(2,1)S(1)} %copy-done.7), channel_id=1, replica_groups=mesh['grp'=2,'section'=16] {'section'}, dimensions={0}, use_global_device_ids=true | all-gather | bytes 104448 | tf_op jit(solution)/shard_map/all_gather | solution.py:131
  32.1 17.9 %all_gather.7 = bf16[768,64]{1,0:T(8,128)(2,1)S(1)} all-gather(bf16[48,64]{1,0:T(8,128)(2,1)S(1)} %copy-done.8), channel_id=1, replica_groups=mesh['grp'=2,'section'=16] {'section'}, dimensions={0}, use_global_device_ids=true | all-gather | bytes 104448 | tf_op jit(solution)/shard_map/all_gather | solution.py:132
  54.7 562.6 %while.25 = (s32[]{:T(128)}, bf16[32,3072]{1,0:T(8,128)(2,1)}, bf16[32,3072]{1,0:T(8,128)(2,1)S(1)}, bf16[1024,768]{0,1:T(8,128)(2,1)}, f32[1024,64]{1,0:T(8,128...) while((s32[]{:T(128)}, bf16[32,3072]{1,0:T(8,128)(2,1)}, ...), condition=%wide.region_12.13_spmd, body=%wide.region_1.12_spmd.sunk | while | flops 2714486016 | bytes 100601624 | solution.py:242
  62.3 9.7 %collective-permute-done.1 = bf16[64,3072]{1,0:T(8,128)(2,1)S(1)} collective-permute-done((bf16[64,3072]{1,0:T(8,128)(2,1)S(1)}, bf16[64,3072]{1,0:T(8,128)(2,1)S(1)}, u32[]{:S(2)}, u32[]{:S(2)}) %collective-permute-start.1) | collective-permute-done | bytes 393248 | tf_op jit(solution)/shard_map/while/body/eval_jaxpr/ppermute | solution.py:20
  73.1 18.2 %collective-permute-done.2 = bf16[128,3072]{1,0:T(8,128)(2,1)} collective-permute-done((bf16[128,3072]{1,0:T(8,128)(2,1)S(1)}, bf16[128,3072]{1,0:T(8,128)(2,1)}, u32[]{:S(2)}, u32[]{:S(2)}) %collective-permute-start.2) | collective-permute-done | bytes 786464 | tf_op jit(solution)/shard_map/while/body/eval_jaxpr/ppermute | solution.py:20
  93.3 25.1 %conditional.2 = (bf16[1024,768]{0,1:T(8,128)(2,1)}, bf16[128,3072]{1,0:T(8,128)(2,1)S(1)}, bf16[128,3072]{1,0:T(8,128)(2,1)S(1)}) conditional(s32[]{:T(128)} %convert_element_type.288, bf16[1024,768]{0,1:T(8,128)(2,1)} %get-tuple-element.1047, (s32[]{:T(128)}, pred[]{:T(512)}, bf16[256,3072]{1,0:T(8,128)(2,1)S(1)}, bf16[256,3072]{1,0:T(8,128)(2,1)S(1)}, ...), branch_computations={%region_2.2_spmd, %region_3.9_spmd} | conditional | flops 2658447616 | bytes 57946768 | solution.py:211
  118.9 17.8 %collective-permute-done.3 = bf16[128,3072]{1,0:T(8,128)(2,1)S(1)} collective-permute-done((bf16[128,3072]{1,0:T(8,128)(2,1)S(1)}, bf16[128,3072]{1,0:T(8,128)(2,1)S(1)}, u32[]{:S(2)}, u32[]{:S(2)}) %collective-permute-start.3) | collective-permute-done | bytes 786464 | tf_op jit(solution)/shard_map/while/body/eval_jaxpr/ppermute | solution.py:20
  165.9 9.5 %collective-permute-done.1 = bf16[64,3072]{1,0:T(8,128)(2,1)S(1)} collective-permute-done((bf16[64,3072]{1,0:T(8,128)(2,1)S(1)}, bf16[64,3072]{1,0:T(8,128)(2,1)S(1)}, u32[]{:S(2)}, u32[]{:S(2)}) %collective-permute-start.1) | collective-permute-done | bytes 393248 | tf_op jit(solution)/shard_map/while/body/eval_jaxpr/ppermute | solution.py:20
  175.5 9.3 %collective-permute-start.2 = (bf16[128,3072]{1,0:T(8,128)(2,1)S(1)}, bf16[128,3072]{1,0:T(8,128)(2,1)}, u32[]{:S(2)}, u32[]{:S(2)}) collective-permute-start(bf16[128,3072]{1,0:T(8,128)(2,1)S(1)} %maximum_select_fusion.6), channel_id=1, source_target_pairs={{0,4},{1,5},{2,6},{3,7},{4,0},{5,1},{6,2},{7,3},{8,12},{9,13},{10,... | collective-permute-start | bytes 2359304 | tf_op jit(solution)/shard_map/while/body/eval_jaxpr/ppermute | solution.py:20
  185.4 16.4 %collective-permute-done.2 = bf16[128,3072]{1,0:T(8,128)(2,1)} collective-permute-done((bf16[128,3072]{1,0:T(8,128)(2,1)S(1)}, bf16[128,3072]{1,0:T(8,128)(2,1)}, u32[]{:S(2)}, u32[]{:S(2)}) %collective-permute-start.2) | collective-permute-done | bytes 786464 | tf_op jit(solution)/shard_map/while/body/eval_jaxpr/ppermute | solution.py:20
  203.9 25.1 %conditional.2 = (bf16[1024,768]{0,1:T(8,128)(2,1)}, bf16[128,3072]{1,0:T(8,128)(2,1)S(1)}, bf16[128,3072]{1,0:T(8,128)(2,1)S(1)}) conditional(s32[]{:T(128)} %convert_element_type.288, bf16[1024,768]{0,1:T(8,128)(2,1)} %get-tuple-element.1047, (s32[]{:T(128)}, pred[]{:T(512)}, bf16[256,3072]{1,0:T(8,128)(2,1)S(1)}, bf16[256,3072]{1,0:T(8,128)(2,1)S(1)}, ...), branch_computations={%region_2.2_spmd, %region_3.9_spmd} | conditional | flops 2658447616 | bytes 57946768 | solution.py:211
  231.0 16.4 %collective-permute-done.3 = bf16[128,3072]{1,0:T(8,128)(2,1)S(1)} collective-permute-done((bf16[128,3072]{1,0:T(8,128)(2,1)S(1)}, bf16[128,3072]{1,0:T(8,128)(2,1)S(1)}, u32[]{:S(2)}, u32[]{:S(2)}) %collective-permute-start.3) | collective-permute-done | bytes 786464 | tf_op jit(solution)/shard_map/while/body/eval_jaxpr/ppermute | solution.py:20
  249.5 7.2 %collective-permute-done.4 = bf16[64,3072]{1,0:T(8,128)(2,1)S(1)} collective-permute-done((bf16[64,3072]{1,0:T(8,128)(2,1)S(1)}, bf16[64,3072]{1,0:T(8,128)(2,1)S(1)}, u32[]{:S(2)}, u32[]{:S(2)}) %collective-permute-start.4) | collective-permute-done | bytes 393248 | tf_op jit(solution)/shard_map/while/body/eval_jaxpr/ppermute | solution.py:20
  280.4 9.5 %collective-permute-done.1 = bf16[64,3072]{1,0:T(8,128)(2,1)S(1)} collective-permute-done((bf16[64,3072]{1,0:T(8,128)(2,1)S(1)}, bf16[64,3072]{1,0:T(8,128)(2,1)S(1)}, u32[]{:S(2)}, u32[]{:S(2)}) %collective-permute-start.1) | collective-permute-done | bytes 393248 | tf_op jit(solution)/shard_map/while/body/eval_jaxpr/ppermute | solution.py:20
  290.0 9.6 %collective-permute-start.2 = (bf16[128,3072]{1,0:T(8,128)(2,1)S(1)}, bf16[128,3072]{1,0:T(8,128)(2,1)}, u32[]{:S(2)}, u32[]{:S(2)}) collective-permute-start(bf16[128,3072]{1,0:T(8,128)(2,1)S(1)} %maximum_select_fusion.6), channel_id=1, source_target_pairs={{0,4},{1,5},{2,6},{3,7},{4,0},{5,1},{6,2},{7,3},{8,12},{9,13},{10,... | collective-permute-start | bytes 2359304 | tf_op jit(solution)/shard_map/while/body/eval_jaxpr/ppermute | solution.py:20
  300.3 16.4 %collective-permute-done.2 = bf16[128,3072]{1,0:T(8,128)(2,1)} collective-permute-done((bf16[128,3072]{1,0:T(8,128)(2,1)S(1)}, bf16[128,3072]{1,0:T(8,128)(2,1)}, u32[]{:S(2)}, u32[]{:S(2)}) %collective-permute-start.2) | collective-permute-done | bytes 786464 | tf_op jit(solution)/shard_map/while/body/eval_jaxpr/ppermute | solution.py:20
  318.8 25.1 %conditional.2 = (bf16[1024,768]{0,1:T(8,128)(2,1)}, bf16[128,3072]{1,0:T(8,128)(2,1)S(1)}, bf16[128,3072]{1,0:T(8,128)(2,1)S(1)}) conditional(s32[]{:T(128)} %convert_element_type.288, bf16[1024,768]{0,1:T(8,128)(2,1)} %get-tuple-element.1047, (s32[]{:T(128)}, pred[]{:T(512)}, bf16[256,3072]{1,0:T(8,128)(2,1)S(1)}, bf16[256,3072]{1,0:T(8,128)(2,1)S(1)}, ...), branch_computations={%region_2.2_spmd, %region_3.9_spmd} | conditional | flops 2658447616 | bytes 57946768 | solution.py:211
  345.8 16.4 %collective-permute-done.3 = bf16[128,3072]{1,0:T(8,128)(2,1)S(1)} collective-permute-done((bf16[128,3072]{1,0:T(8,128)(2,1)S(1)}, bf16[128,3072]{1,0:T(8,128)(2,1)S(1)}, u32[]{:S(2)}, u32[]{:S(2)}) %collective-permute-start.3) | collective-permute-done | bytes 786464 | tf_op jit(solution)/shard_map/while/body/eval_jaxpr/ppermute | solution.py:20
  364.4 7.2 %collective-permute-done.4 = bf16[64,3072]{1,0:T(8,128)(2,1)S(1)} collective-permute-done((bf16[64,3072]{1,0:T(8,128)(2,1)S(1)}, bf16[64,3072]{1,0:T(8,128)(2,1)S(1)}, u32[]{:S(2)}, u32[]{:S(2)}) %collective-permute-start.4) | collective-permute-done | bytes 393248 | tf_op jit(solution)/shard_map/while/body/eval_jaxpr/ppermute | solution.py:20
  395.2 9.5 %collective-permute-done.1 = bf16[64,3072]{1,0:T(8,128)(2,1)S(1)} collective-permute-done((bf16[64,3072]{1,0:T(8,128)(2,1)S(1)}, bf16[64,3072]{1,0:T(8,128)(2,1)S(1)}, u32[]{:S(2)}, u32[]{:S(2)}) %collective-permute-start.1) | collective-permute-done | bytes 393248 | tf_op jit(solution)/shard_map/while/body/eval_jaxpr/ppermute | solution.py:20
  404.9 9.6 %collective-permute-start.2 = (bf16[128,3072]{1,0:T(8,128)(2,1)S(1)}, bf16[128,3072]{1,0:T(8,128)(2,1)}, u32[]{:S(2)}, u32[]{:S(2)}) collective-permute-start(bf16[128,3072]{1,0:T(8,128)(2,1)S(1)} %maximum_select_fusion.6), channel_id=1, source_target_pairs={{0,4},{1,5},{2,6},{3,7},{4,0},{5,1},{6,2},{7,3},{8,12},{9,13},{10,... | collective-permute-start | bytes 2359304 | tf_op jit(solution)/shard_map/while/body/eval_jaxpr/ppermute | solution.py:20
  415.1 16.4 %collective-permute-done.2 = bf16[128,3072]{1,0:T(8,128)(2,1)} collective-permute-done((bf16[128,3072]{1,0:T(8,128)(2,1)S(1)}, bf16[128,3072]{1,0:T(8,128)(2,1)}, u32[]{:S(2)}, u32[]{:S(2)}) %collective-permute-start.2) | collective-permute-done | bytes 786464 | tf_op jit(solution)/shard_map/while/body/eval_jaxpr/ppermute | solution.py:20
  433.6 25.2 %conditional.2 = (bf16[1024,768]{0,1:T(8,128)(2,1)}, bf16[128,3072]{1,0:T(8,128)(2,1)S(1)}, bf16[128,3072]{1,0:T(8,128)(2,1)S(1)}) conditional(s32[]{:T(128)} %convert_element_type.288, bf16[1024,768]{0,1:T(8,128)(2,1)} %get-tuple-element.1047, (s32[]{:T(128)}, pred[]{:T(512)}, bf16[256,3072]{1,0:T(8,128)(2,1)S(1)}, bf16[256,3072]{1,0:T(8,128)(2,1)S(1)}, ...), branch_computations={%region_2.2_spmd, %region_3.9_spmd} | conditional | flops 2658447616 | bytes 57946768 | solution.py:211
  460.7 16.4 %collective-permute-done.3 = bf16[128,3072]{1,0:T(8,128)(2,1)S(1)} collective-permute-done((bf16[128,3072]{1,0:T(8,128)(2,1)S(1)}, bf16[128,3072]{1,0:T(8,128)(2,1)S(1)}, u32[]{:S(2)}, u32[]{:S(2)}) %collective-permute-start.3) | collective-permute-done | bytes 786464 | tf_op jit(solution)/shard_map/while/body/eval_jaxpr/ppermute | solution.py:20
  479.3 7.2 %collective-permute-done.4 = bf16[64,3072]{1,0:T(8,128)(2,1)S(1)} collective-permute-done((bf16[64,3072]{1,0:T(8,128)(2,1)S(1)}, bf16[64,3072]{1,0:T(8,128)(2,1)S(1)}, u32[]{:S(2)}, u32[]{:S(2)}) %collective-permute-start.4) | collective-permute-done | bytes 393248 | tf_op jit(solution)/shard_map/while/body/eval_jaxpr/ppermute | solution.py:20
  510.1 9.5 %collective-permute-done.1 = bf16[64,3072]{1,0:T(8,128)(2,1)S(1)} collective-permute-done((bf16[64,3072]{1,0:T(8,128)(2,1)S(1)}, bf16[64,3072]{1,0:T(8,128)(2,1)S(1)}, u32[]{:S(2)}, u32[]{:S(2)}) %collective-permute-start.1) | collective-permute-done | bytes 393248 | tf_op jit(solution)/shard_map/while/body/eval_jaxpr/ppermute | solution.py:20
  519.7 9.6 %collective-permute-start.2 = (bf16[128,3072]{1,0:T(8,128)(2,1)S(1)}, bf16[128,3072]{1,0:T(8,128)(2,1)}, u32[]{:S(2)}, u32[]{:S(2)}) collective-permute-start(bf16[128,3072]{1,0:T(8,128)(2,1)S(1)} %maximum_select_fusion.6), channel_id=1, source_target_pairs={{0,4},{1,5},{2,6},{3,7},{4,0},{5,1},{6,2},{7,3},{8,12},{9,13},{10,... | collective-permute-start | bytes 2359304 | tf_op jit(solution)/shard_map/while/body/eval_jaxpr/ppermute | solution.py:20
  530.0 16.4 %collective-permute-done.2 = bf16[128,3072]{1,0:T(8,128)(2,1)} collective-permute-done((bf16[128,3072]{1,0:T(8,128)(2,1)S(1)}, bf16[128,3072]{1,0:T(8,128)(2,1)}, u32[]{:S(2)}, u32[]{:S(2)}) %collective-permute-start.2) | collective-permute-done | bytes 786464 | tf_op jit(solution)/shard_map/while/body/eval_jaxpr/ppermute | solution.py:20
  550.6 16.4 %collective-permute-done.3 = bf16[128,3072]{1,0:T(8,128)(2,1)S(1)} collective-permute-done((bf16[128,3072]{1,0:T(8,128)(2,1)S(1)}, bf16[128,3072]{1,0:T(8,128)(2,1)S(1)}, u32[]{:S(2)}, u32[]{:S(2)}) %collective-permute-start.3) | collective-permute-done | bytes 786464 | tf_op jit(solution)/shard_map/while/body/eval_jaxpr/ppermute | solution.py:20
  569.1 7.2 %collective-permute-done.4 = bf16[64,3072]{1,0:T(8,128)(2,1)S(1)} collective-permute-done((bf16[64,3072]{1,0:T(8,128)(2,1)S(1)}, bf16[64,3072]{1,0:T(8,128)(2,1)S(1)}, u32[]{:S(2)}, u32[]{:S(2)}) %collective-permute-start.4) | collective-permute-done | bytes 393248 | tf_op jit(solution)/shard_map/while/body/eval_jaxpr/ppermute | solution.py:20
  578.3 31.0 %collective-permute-start.6 = (bf16[32,3072]{1,0:T(8,128)(2,1)S(1)}, bf16[32,3072]{1,0:T(8,128)(2,1)}, u32[]{:S(2)}, u32[]{:S(2)}) collective-permute-start(bf16[32,3072]{1,0:T(8,128)(2,1)S(1)} %get-tuple-element.999), channel_id=1, source_target_pairs={{0,8},{1,9},{2,10},{3,11},{4,12},{5,13},{6,14},{7,15},{16,24},{17,... | collective-permute-start | bytes 589832 | tf_op jit(solution)/shard_map/while/body/eval_jaxpr/ppermute | solution.py:26
  619.1 66.3 %reduce-scatter.2.cloned.1.call-done = f32[48,64]{1,0:T(8,128)} async-done(((f32[768,64]{1,0:T(8,128)}), f32[48,64]{1,0:T(8,128)}) %reduce-scatter.2.cloned.1.call-update) | async-done | bytes 12304 | tf_op jit(solution)/shard_map/reduce_scatter | solution.py:243
  (394 shorter events, 245.0 us)
Async XLA Ops:
  6.6 678.8 %reduce-scatter.2.cloned.1.call-start = ((), (), s32[]{:S(2)}) async-start(), calls=%async_computation.1 | async-start | bytes 417792 | tf_op jit(solution)/shard_map/reduce_scatter | solution.py:243
  60.6 11.4 %collective-permute-start.1 = (bf16[64,3072]{1,0:T(8,128)(2,1)S(1)}, bf16[64,3072]{1,0:T(8,128)(2,1)S(1)}, u32[]{:S(2)}, u32[]{:S(2)}) collective-permute-start(bf16[64,3072]{1,0:T(8,128)(2,1)S(1)} %maximum_select_fusion.5), channel_id=1, source_target_pairs={{0,2},{1,3},{2,0},{3,1},{4,6},{5,7},{6,4},{7,5},{8,10},{9,11},{10,... | collective-permute-start | bytes 1179656 | tf_op jit(solution)/shard_map/while/body/eval_jaxpr/ppermute | solution.py:20
  72.2 19.1 %collective-permute-start.2 = (bf16[128,3072]{1,0:T(8,128)(2,1)S(1)}, bf16[128,3072]{1,0:T(8,128)(2,1)}, u32[]{:S(2)}, u32[]{:S(2)}) collective-permute-start(bf16[128,3072]{1,0:T(8,128)(2,1)S(1)} %maximum_select_fusion.6), channel_id=1, source_target_pairs={{0,4},{1,5},{2,6},{3,7},{4,0},{5,1},{6,2},{7,3},{8,12},{9,13},{10,... | collective-permute-start | bytes 2359304 | tf_op jit(solution)/shard_map/while/body/eval_jaxpr/ppermute | solution.py:20
  118.6 18.1 %collective-permute-start.3 = (bf16[128,3072]{1,0:T(8,128)(2,1)S(1)}, bf16[128,3072]{1,0:T(8,128)(2,1)S(1)}, u32[]{:S(2)}, u32[]{:S(2)}) collective-permute-start(bf16[128,3072]{1,0:T(8,128)(2,1)S(1)} %broadcast_select_fusion.7), channel_id=1, source_target_pairs={{0,4},{1,5},{2,6},{3,7},{4,0},{5,1},{6,2},{7,3},{8,12},{9,13},{10,... | collective-permute-start | bytes 2359304 | tf_op jit(solution)/shard_map/while/body/eval_jaxpr/ppermute | solution.py:20
  137.1 8.9 %collective-permute-start.4 = (bf16[64,3072]{1,0:T(8,128)(2,1)S(1)}, bf16[64,3072]{1,0:T(8,128)(2,1)S(1)}, u32[]{:S(2)}, u32[]{:S(2)}) collective-permute-start(bf16[64,3072]{1,0:T(8,128)(2,1)S(1)} %select_convert_fusion.4), channel_id=1, source_target_pairs={{0,2},{1,3},{2,0},{3,1},{4,6},{5,7},{6,4},{7,5},{8,10},{9,11},{10,... | collective-permute-start | bytes 1179656 | tf_op jit(solution)/shard_map/while/body/eval_jaxpr/ppermute | solution.py:20
  147.9 6.6 collective-permute-start.6
  150.0 8.2 %collective-permute-start.7 = (bf16[32,3072]{1,0:T(8,128)(2,1)S(1)}, bf16[32,3072]{1,0:T(8,128)(2,1)S(1)}, u32[]{:S(2)}, u32[]{:S(2)}) collective-permute-start(bf16[32,3072]{1,0:T(8,128)(2,1)S(1)} %convert_select_fusion.4), channel_id=1, source_target_pairs={{0,8},{1,9},{2,10},{3,11},{4,12},{5,13},{6,14},{7,15},{16,24},{17,... | collective-permute-start | bytes 589832 | tf_op jit(solution)/shard_map/while/body/eval_jaxpr/ppermute | solution.py:26
  164.1 11.2 %collective-permute-start.1 = (bf16[64,3072]{1,0:T(8,128)(2,1)S(1)}, bf16[64,3072]{1,0:T(8,128)(2,1)S(1)}, u32[]{:S(2)}, u32[]{:S(2)}) collective-permute-start(bf16[64,3072]{1,0:T(8,128)(2,1)S(1)} %maximum_select_fusion.5), channel_id=1, source_target_pairs={{0,2},{1,3},{2,0},{3,1},{4,6},{5,7},{6,4},{7,5},{8,10},{9,11},{10,... | collective-permute-start | bytes 1179656 | tf_op jit(solution)/shard_map/while/body/eval_jaxpr/ppermute | solution.py:20
  175.5 26.4 %collective-permute-start.2 = (bf16[128,3072]{1,0:T(8,128)(2,1)S(1)}, bf16[128,3072]{1,0:T(8,128)(2,1)}, u32[]{:S(2)}, u32[]{:S(2)}) collective-permute-start(bf16[128,3072]{1,0:T(8,128)(2,1)S(1)} %maximum_select_fusion.6), channel_id=1, source_target_pairs={{0,4},{1,5},{2,6},{3,7},{4,0},{5,1},{6,2},{7,3},{8,12},{9,13},{10,... | collective-permute-start | bytes 2359304 | tf_op jit(solution)/shard_map/while/body/eval_jaxpr/ppermute | solution.py:20
  229.2 18.2 %collective-permute-start.3 = (bf16[128,3072]{1,0:T(8,128)(2,1)S(1)}, bf16[128,3072]{1,0:T(8,128)(2,1)S(1)}, u32[]{:S(2)}, u32[]{:S(2)}) collective-permute-start(bf16[128,3072]{1,0:T(8,128)(2,1)S(1)} %broadcast_select_fusion.7), channel_id=1, source_target_pairs={{0,4},{1,5},{2,6},{3,7},{4,0},{5,1},{6,2},{7,3},{8,12},{9,13},{10,... | collective-permute-start | bytes 2359304 | tf_op jit(solution)/shard_map/while/body/eval_jaxpr/ppermute | solution.py:20
  247.8 8.9 %collective-permute-start.4 = (bf16[64,3072]{1,0:T(8,128)(2,1)S(1)}, bf16[64,3072]{1,0:T(8,128)(2,1)S(1)}, u32[]{:S(2)}, u32[]{:S(2)}) collective-permute-start(bf16[64,3072]{1,0:T(8,128)(2,1)S(1)} %select_convert_fusion.4), channel_id=1, source_target_pairs={{0,2},{1,3},{2,0},{3,1},{4,6},{5,7},{6,4},{7,5},{8,10},{9,11},{10,... | collective-permute-start | bytes 1179656 | tf_op jit(solution)/shard_map/while/body/eval_jaxpr/ppermute | solution.py:20
  258.7 10.7 %collective-permute-start.6 = (bf16[32,3072]{1,0:T(8,128)(2,1)S(1)}, bf16[32,3072]{1,0:T(8,128)(2,1)}, u32[]{:S(2)}, u32[]{:S(2)}) collective-permute-start(bf16[32,3072]{1,0:T(8,128)(2,1)S(1)} %get-tuple-element.999), channel_id=1, source_target_pairs={{0,8},{1,9},{2,10},{3,11},{4,12},{5,13},{6,14},{7,15},{16,24},{17,... | collective-permute-start | bytes 589832 | tf_op jit(solution)/shard_map/while/body/eval_jaxpr/ppermute | solution.py:26
  264.8 7.9 %collective-permute-start.7 = (bf16[32,3072]{1,0:T(8,128)(2,1)S(1)}, bf16[32,3072]{1,0:T(8,128)(2,1)S(1)}, u32[]{:S(2)}, u32[]{:S(2)}) collective-permute-start(bf16[32,3072]{1,0:T(8,128)(2,1)S(1)} %convert_select_fusion.4), channel_id=1, source_target_pairs={{0,8},{1,9},{2,10},{3,11},{4,12},{5,13},{6,14},{7,15},{16,24},{17,... | collective-permute-start | bytes 589832 | tf_op jit(solution)/shard_map/while/body/eval_jaxpr/ppermute | solution.py:26
  278.6 11.2 %collective-permute-start.1 = (bf16[64,3072]{1,0:T(8,128)(2,1)S(1)}, bf16[64,3072]{1,0:T(8,128)(2,1)S(1)}, u32[]{:S(2)}, u32[]{:S(2)}) collective-permute-start(bf16[64,3072]{1,0:T(8,128)(2,1)S(1)} %maximum_select_fusion.5), channel_id=1, source_target_pairs={{0,2},{1,3},{2,0},{3,1},{4,6},{5,7},{6,4},{7,5},{8,10},{9,11},{10,... | collective-permute-start | bytes 1179656 | tf_op jit(solution)/shard_map/while/body/eval_jaxpr/ppermute | solution.py:20
  290.0 26.7 %collective-permute-start.2 = (bf16[128,3072]{1,0:T(8,128)(2,1)S(1)}, bf16[128,3072]{1,0:T(8,128)(2,1)}, u32[]{:S(2)}, u32[]{:S(2)}) collective-permute-start(bf16[128,3072]{1,0:T(8,128)(2,1)S(1)} %maximum_select_fusion.6), channel_id=1, source_target_pairs={{0,4},{1,5},{2,6},{3,7},{4,0},{5,1},{6,2},{7,3},{8,12},{9,13},{10,... | collective-permute-start | bytes 2359304 | tf_op jit(solution)/shard_map/while/body/eval_jaxpr/ppermute | solution.py:20
  344.0 18.2 %collective-permute-start.3 = (bf16[128,3072]{1,0:T(8,128)(2,1)S(1)}, bf16[128,3072]{1,0:T(8,128)(2,1)S(1)}, u32[]{:S(2)}, u32[]{:S(2)}) collective-permute-start(bf16[128,3072]{1,0:T(8,128)(2,1)S(1)} %broadcast_select_fusion.7), channel_id=1, source_target_pairs={{0,4},{1,5},{2,6},{3,7},{4,0},{5,1},{6,2},{7,3},{8,12},{9,13},{10,... | collective-permute-start | bytes 2359304 | tf_op jit(solution)/shard_map/while/body/eval_jaxpr/ppermute | solution.py:20
  362.6 8.9 %collective-permute-start.4 = (bf16[64,3072]{1,0:T(8,128)(2,1)S(1)}, bf16[64,3072]{1,0:T(8,128)(2,1)S(1)}, u32[]{:S(2)}, u32[]{:S(2)}) collective-permute-start(bf16[64,3072]{1,0:T(8,128)(2,1)S(1)} %select_convert_fusion.4), channel_id=1, source_target_pairs={{0,2},{1,3},{2,0},{3,1},{4,6},{5,7},{6,4},{7,5},{8,10},{9,11},{10,... | collective-permute-start | bytes 1179656 | tf_op jit(solution)/shard_map/while/body/eval_jaxpr/ppermute | solution.py:20
  373.5 10.6 %collective-permute-start.6 = (bf16[32,3072]{1,0:T(8,128)(2,1)S(1)}, bf16[32,3072]{1,0:T(8,128)(2,1)}, u32[]{:S(2)}, u32[]{:S(2)}) collective-permute-start(bf16[32,3072]{1,0:T(8,128)(2,1)S(1)} %get-tuple-element.999), channel_id=1, source_target_pairs={{0,8},{1,9},{2,10},{3,11},{4,12},{5,13},{6,14},{7,15},{16,24},{17,... | collective-permute-start | bytes 589832 | tf_op jit(solution)/shard_map/while/body/eval_jaxpr/ppermute | solution.py:26
  379.7 7.9 %collective-permute-start.7 = (bf16[32,3072]{1,0:T(8,128)(2,1)S(1)}, bf16[32,3072]{1,0:T(8,128)(2,1)S(1)}, u32[]{:S(2)}, u32[]{:S(2)}) collective-permute-start(bf16[32,3072]{1,0:T(8,128)(2,1)S(1)} %convert_select_fusion.4), channel_id=1, source_target_pairs={{0,8},{1,9},{2,10},{3,11},{4,12},{5,13},{6,14},{7,15},{16,24},{17,... | collective-permute-start | bytes 589832 | tf_op jit(solution)/shard_map/while/body/eval_jaxpr/ppermute | solution.py:26
  393.5 11.2 %collective-permute-start.1 = (bf16[64,3072]{1,0:T(8,128)(2,1)S(1)}, bf16[64,3072]{1,0:T(8,128)(2,1)S(1)}, u32[]{:S(2)}, u32[]{:S(2)}) collective-permute-start(bf16[64,3072]{1,0:T(8,128)(2,1)S(1)} %maximum_select_fusion.5), channel_id=1, source_target_pairs={{0,2},{1,3},{2,0},{3,1},{4,6},{5,7},{6,4},{7,5},{8,10},{9,11},{10,... | collective-permute-start | bytes 1179656 | tf_op jit(solution)/shard_map/while/body/eval_jaxpr/ppermute | solution.py:20
  404.9 26.7 %collective-permute-start.2 = (bf16[128,3072]{1,0:T(8,128)(2,1)S(1)}, bf16[128,3072]{1,0:T(8,128)(2,1)}, u32[]{:S(2)}, u32[]{:S(2)}) collective-permute-start(bf16[128,3072]{1,0:T(8,128)(2,1)S(1)} %maximum_select_fusion.6), channel_id=1, source_target_pairs={{0,4},{1,5},{2,6},{3,7},{4,0},{5,1},{6,2},{7,3},{8,12},{9,13},{10,... | collective-permute-start | bytes 2359304 | tf_op jit(solution)/shard_map/while/body/eval_jaxpr/ppermute | solution.py:20
  458.9 18.2 %collective-permute-start.3 = (bf16[128,3072]{1,0:T(8,128)(2,1)S(1)}, bf16[128,3072]{1,0:T(8,128)(2,1)S(1)}, u32[]{:S(2)}, u32[]{:S(2)}) collective-permute-start(bf16[128,3072]{1,0:T(8,128)(2,1)S(1)} %broadcast_select_fusion.7), channel_id=1, source_target_pairs={{0,4},{1,5},{2,6},{3,7},{4,0},{5,1},{6,2},{7,3},{8,12},{9,13},{10,... | collective-permute-start | bytes 2359304 | tf_op jit(solution)/shard_map/while/body/eval_jaxpr/ppermute | solution.py:20
  477.5 8.9 %collective-permute-start.4 = (bf16[64,3072]{1,0:T(8,128)(2,1)S(1)}, bf16[64,3072]{1,0:T(8,128)(2,1)S(1)}, u32[]{:S(2)}, u32[]{:S(2)}) collective-permute-start(bf16[64,3072]{1,0:T(8,128)(2,1)S(1)} %select_convert_fusion.4), channel_id=1, source_target_pairs={{0,2},{1,3},{2,0},{3,1},{4,6},{5,7},{6,4},{7,5},{8,10},{9,11},{10,... | collective-permute-start | bytes 1179656 | tf_op jit(solution)/shard_map/while/body/eval_jaxpr/ppermute | solution.py:20
  488.4 10.6 %collective-permute-start.6 = (bf16[32,3072]{1,0:T(8,128)(2,1)S(1)}, bf16[32,3072]{1,0:T(8,128)(2,1)}, u32[]{:S(2)}, u32[]{:S(2)}) collective-permute-start(bf16[32,3072]{1,0:T(8,128)(2,1)S(1)} %get-tuple-element.999), channel_id=1, source_target_pairs={{0,8},{1,9},{2,10},{3,11},{4,12},{5,13},{6,14},{7,15},{16,24},{17,... | collective-permute-start | bytes 589832 | tf_op jit(solution)/shard_map/while/body/eval_jaxpr/ppermute | solution.py:26
  494.5 7.9 %collective-permute-start.7 = (bf16[32,3072]{1,0:T(8,128)(2,1)S(1)}, bf16[32,3072]{1,0:T(8,128)(2,1)S(1)}, u32[]{:S(2)}, u32[]{:S(2)}) collective-permute-start(bf16[32,3072]{1,0:T(8,128)(2,1)S(1)} %convert_select_fusion.4), channel_id=1, source_target_pairs={{0,8},{1,9},{2,10},{3,11},{4,12},{5,13},{6,14},{7,15},{16,24},{17,... | collective-permute-start | bytes 589832 | tf_op jit(solution)/shard_map/while/body/eval_jaxpr/ppermute | solution.py:26
  508.3 11.2 %collective-permute-start.1 = (bf16[64,3072]{1,0:T(8,128)(2,1)S(1)}, bf16[64,3072]{1,0:T(8,128)(2,1)S(1)}, u32[]{:S(2)}, u32[]{:S(2)}) collective-permute-start(bf16[64,3072]{1,0:T(8,128)(2,1)S(1)} %maximum_select_fusion.5), channel_id=1, source_target_pairs={{0,2},{1,3},{2,0},{3,1},{4,6},{5,7},{6,4},{7,5},{8,10},{9,11},{10,... | collective-permute-start | bytes 1179656 | tf_op jit(solution)/shard_map/while/body/eval_jaxpr/ppermute | solution.py:20
  519.7 26.7 %collective-permute-start.2 = (bf16[128,3072]{1,0:T(8,128)(2,1)S(1)}, bf16[128,3072]{1,0:T(8,128)(2,1)}, u32[]{:S(2)}, u32[]{:S(2)}) collective-permute-start(bf16[128,3072]{1,0:T(8,128)(2,1)S(1)} %maximum_select_fusion.6), channel_id=1, source_target_pairs={{0,4},{1,5},{2,6},{3,7},{4,0},{5,1},{6,2},{7,3},{8,12},{9,13},{10,... | collective-permute-start | bytes 2359304 | tf_op jit(solution)/shard_map/while/body/eval_jaxpr/ppermute | solution.py:20
  548.8 18.2 %collective-permute-start.3 = (bf16[128,3072]{1,0:T(8,128)(2,1)S(1)}, bf16[128,3072]{1,0:T(8,128)(2,1)S(1)}, u32[]{:S(2)}, u32[]{:S(2)}) collective-permute-start(bf16[128,3072]{1,0:T(8,128)(2,1)S(1)} %broadcast_select_fusion.7), channel_id=1, source_target_pairs={{0,4},{1,5},{2,6},{3,7},{4,0},{5,1},{6,2},{7,3},{8,12},{9,13},{10,... | collective-permute-start | bytes 2359304 | tf_op jit(solution)/shard_map/while/body/eval_jaxpr/ppermute | solution.py:20
  567.4 8.9 %collective-permute-start.4 = (bf16[64,3072]{1,0:T(8,128)(2,1)S(1)}, bf16[64,3072]{1,0:T(8,128)(2,1)S(1)}, u32[]{:S(2)}, u32[]{:S(2)}) collective-permute-start(bf16[64,3072]{1,0:T(8,128)(2,1)S(1)} %select_convert_fusion.4), channel_id=1, source_target_pairs={{0,2},{1,3},{2,0},{3,1},{4,6},{5,7},{6,4},{7,5},{8,10},{9,11},{10,... | collective-permute-start | bytes 1179656 | tf_op jit(solution)/shard_map/while/body/eval_jaxpr/ppermute | solution.py:20
  576.5 1.5 collective-permute-start.5
  578.3 35.6 %collective-permute-start.6 = (bf16[32,3072]{1,0:T(8,128)(2,1)S(1)}, bf16[32,3072]{1,0:T(8,128)(2,1)}, u32[]{:S(2)}, u32[]{:S(2)}) collective-permute-start(bf16[32,3072]{1,0:T(8,128)(2,1)S(1)} %get-tuple-element.999), channel_id=1, source_target_pairs={{0,8},{1,9},{2,10},{3,11},{4,12},{5,13},{6,14},{7,15},{16,24},{17,... | collective-permute-start | bytes 589832 | tf_op jit(solution)/shard_map/while/body/eval_jaxpr/ppermute | solution.py:26
  609.4 7.9 %collective-permute-start.7 = (bf16[32,3072]{1,0:T(8,128)(2,1)S(1)}, bf16[32,3072]{1,0:T(8,128)(2,1)S(1)}, u32[]{:S(2)}, u32[]{:S(2)}) collective-permute-start(bf16[32,3072]{1,0:T(8,128)(2,1)S(1)} %convert_select_fusion.4), channel_id=1, source_target_pairs={{0,8},{1,9},{2,10},{3,11},{4,12},{5,13},{6,14},{7,15},{16,24},{17,... | collective-permute-start | bytes 589832 | tf_op jit(solution)/shard_map/while/body/eval_jaxpr/ppermute | solution.py:26
  (41 other events, 397.6 us)
Sparse Core Ops, SparseCore 0:
  619.2 66.1 reduce-scatter.1
where the time goes:
time: 694 us; the launch traced here: 692 us
  waiting for transfers between devices  351 us (51%)
  starting transfers between devices  121 us (17%)
  matrix products  75.3 us (11%)
  blocking collectives  41.6 us (6%)
  local copies, waits for them, and re-layouts  38.4 us (6%)
  other arithmetic  37.4 us (5%)
  between operations  13.5 us (2%)
  loops' own time  13 us (2%)
    ppermute x30, waiting for transfers between devices, from_partner(): lax.ppermute(value, axis, [(i, i ^ 1 << distance) for i in range(lax.axis...  261 us
    reduce_scatter x1, waiting for transfers between devices, on_device(): lax.psum_scatter(finished[3][:seq_rows], 'section', scatter_dimension=0,...  66.3 us
    ppermute x30, starting transfers between devices, from_partner(): lax.ppermute(value, axis, [(i, i ^ 1 << distance) for i in range(lax.axis...  64 us
    ppermute x10, starting transfers between devices, from_behind(): lax.ppermute(value, axis, [(source, source + steps) for source in range(l...  57.5 us
    dot_general x4, matrix products, attend_group(): jnp.dot(modded, w_qkv, preferred_element_type=jnp.float32)  24.9 us
    ppermute x10, waiting for transfers between devices, from_behind(): lax.ppermute(value, axis, [(source, source + steps) for source in range(l...  23.8 us
    all_gather x1, blocking collectives, on_device(): lax.all_gather(latent, 'section', axis=0, tiled=True)  23.6 us
    all_gather x1, blocking collectives, on_device(): lax.all_gather(control_latent, 'section', axis=0, tiled=True)  17.9 us
  transfers between devices with their start and end apart: 41, of which 41 were waited for; matrix products, arithmetic and copies ran while one was open for 2% of the time, Pallas kernels for 0%

commit v1 on v0

--- a/solution.py
+++ b/solution.py
@@ -3,6 +3,7 @@
 import jax.numpy as jnp
 from jax import lax
 from jax.sharding import PartitionSpec as P
+from jax.lax import axis_index, axis_size, ppermute
 
 D = 3072
 HD = 128
@@ -14,6 +15,22 @@
 TILES = 6
 PMAX = 2
 EPSILON = 1e-06
+
+
+def sample_direct(piece_in, dim_at):
+    wide_out = axis_size("section")
+    main, reply = (wide_out, axis_index("section"))
+    current_value, upper = (piece_in, 1)
+    while upper < main:
+        store = []
+        for hop_no in range(main):
+            store.append((hop_no, hop_no ^ upper))
+        v1 = ppermute(current_value, axis_name="section", perm=store)
+        block_out = jnp.concatenate([current_value, v1], axis=dim_at)
+        block_next = jnp.concatenate([v1, current_value], axis=dim_at)
+        current_value = jnp.where(reply & upper == 0, block_out, block_next)
+        upper = 2 * upper
+    return current_value
 
 
 def from_partner(value, axis, distance):
@@ -129,7 +146,7 @@
         share_start = share_start + (group_index >> bit_index & 1) * (row_count >> position + 1)
     whole_latent, whole_control = (
         lax.all_gather(latent, "section", axis=0, tiled=True),
-        lax.all_gather(control_latent, "section", axis=0, tiled=True),
+        sample_direct(control_latent, 0),
     )
     padding = ((0, row_count), (0, 0))
     latent_pad = jnp.pad(whole_latent, padding)

time: 694 us -> 686 us (0.988)
  blocking collectives: 41.6 us -> 20.1 us
  waiting for transfers between devices: 351 us -> 360 us
    all_gather x1 -> x0, blocking collectives: 17.9 us -> none  [on_device(): lax.all_gather(control_latent, 'section', axis=0, tiled=True)]
    ppermute x0 -> x4, starting transfers between devices: none -> 8.32 us  [sample_direct(): v1 = ppermute(current_value, axis_name='section', perm=store)]
  transfers between devices with their start and end apart: 41 -> 45, of which waited for: 41 -> 43; matrix products, arithmetic and copies ran while one was open for 2% -> 3% of each run, Pallas kernels for 0% -> 0%
where the time goes in v1:
time: 686 us; the launch traced here: 684 us
  waiting for transfers between devices  360 us (52%)
  starting transfers between devices  123 us (18%)
  matrix products  74.9 us (11%)
  local copies, waits for them, and re-layouts  40.3 us (6%)
  other arithmetic  39.6 us (6%)
  blocking collectives  20.1 us (3%)
  between operations  13.5 us (2%)
  loops' own time  13.1 us (2%)
    ppermute x30, waiting for transfers between devices, from_partner(): lax.ppermute(value, axis, [(i, i ^ 1 << distance) for i in range(lax.axis...  268 us
    reduce_scatter x1, waiting for transfers between devices, on_device(): lax.psum_scatter(finished[3][:seq_rows], 'section', scatter_dimension=0,...  65.7 us
    ppermute x10, starting transfers between devices, from_behind(): lax.ppermute(value, axis, [(source, source + steps) for source in range(l...  57.3 us
    ppermute x30, starting transfers between devices, from_partner(): lax.ppermute(value, axis, [(i, i ^ 1 << distance) for i in range(lax.axis...  57.1 us
    dot_general x4, matrix products, attend_group(): jnp.dot(modded, w_qkv, preferred_element_type=jnp.float32)  24.5 us
    ppermute x10, waiting for transfers between devices, from_behind(): lax.ppermute(value, axis, [(source, source + steps) for source in range(l...  23.8 us
    all_gather x1, blocking collectives, on_device(): lax.all_gather(latent, 'section', axis=0, tiled=True)  20.1 us
    dot_general x4, matrix products, attend_group(): jnp.einsum('thqk,tkhd->tqhd', probabilities, value_rows, preferred_elemen...  14 us
  transfers between devices with their start and end apart: 45, of which 43 were waited for; matrix products, arithmetic and copies ran while one was open for 3% of the time, Pallas kernels for 0%

profile of v1, /device:TPU:0, one launch (start us, length us, event | category | flops | bytes accessed | tf_op | source)
XLA Modules:
  0.0 684.5 jit_solution(920171735411542106)
XLA Ops:
  24.9 20.1 %all_gather.3 = bf16[768,64]{1,0:T(8,128)(2,1)S(1)} all-gather(bf16[48,64]{1,0:T(8,128)(2,1)S(1)} %copy-done.7), channel_id=1, replica_groups=mesh['grp'=2,'section'=16] {'section'}, dimensions={0}, use_global_device_ids=true | all-gather | bytes 104448 | tf_op jit(solution)/shard_map/all_gather | solution.py:148
  48.1 562.0 %while.25 = (s32[]{:T(128)}, bf16[32,3072]{1,0:T(8,128)(2,1)}, bf16[32,3072]{1,0:T(8,128)(2,1)S(1)}, bf16[1024,768]{0,1:T(8,128)(2,1)}, f32[1024,64]{1,0:T(8,128...) while((s32[]{:T(128)}, bf16[32,3072]{1,0:T(8,128)(2,1)}, ...), condition=%wide.region_12.13_spmd, body=%wide.region_1.12_spmd.sunk | while | flops 2714486016 | bytes 100601624 | solution.py:259
  54.1 11.4 %collective-permute-done.1 = bf16[64,3072]{1,0:T(8,128)(2,1)S(1)} collective-permute-done((bf16[64,3072]{1,0:T(8,128)(2,1)S(1)}, bf16[64,3072]{1,0:T(8,128)(2,1)S(1)}, u32[]{:S(2)}, u32[]{:S(2)}) %collective-permute-start.1) | collective-permute-done | bytes 393248 | tf_op jit(solution)/shard_map/while/body/eval_jaxpr/ppermute | solution.py:37
  66.5 18.2 %collective-permute-done.2 = bf16[128,3072]{1,0:T(8,128)(2,1)} collective-permute-done((bf16[128,3072]{1,0:T(8,128)(2,1)S(1)}, bf16[128,3072]{1,0:T(8,128)(2,1)}, u32[]{:S(2)}, u32[]{:S(2)}) %collective-permute-start.2) | collective-permute-done | bytes 786464 | tf_op jit(solution)/shard_map/while/body/eval_jaxpr/ppermute | solution.py:37
  86.8 25.0 %conditional.2 = (bf16[1024,768]{0,1:T(8,128)(2,1)}, bf16[128,3072]{1,0:T(8,128)(2,1)S(1)}, bf16[128,3072]{1,0:T(8,128)(2,1)S(1)}) conditional(s32[]{:T(128)} %convert_element_type.288, bf16[1024,768]{0,1:T(8,128)(2,1)} %get-tuple-element.1047, (s32[]{:T(128)}, pred[]{:T(512)}, bf16[256,3072]{1,0:T(8,128)(2,1)S(1)}, bf16[256,3072]{1,0:T(8,128)(2,1)S(1)}, ...), branch_computations={%region_2.2_spmd, %region_3.9_spmd} | conditional | flops 2658447616 | bytes 57946768 | solution.py:228
  112.2 17.8 %collective-permute-done.3 = bf16[128,3072]{1,0:T(8,128)(2,1)S(1)} collective-permute-done((bf16[128,3072]{1,0:T(8,128)(2,1)S(1)}, bf16[128,3072]{1,0:T(8,128)(2,1)S(1)}, u32[]{:S(2)}, u32[]{:S(2)}) %collective-permute-start.3) | collective-permute-done | bytes 786464 | tf_op jit(solution)/shard_map/while/body/eval_jaxpr/ppermute | solution.py:37
  131.3 7.9 %collective-permute-done.4 = bf16[64,3072]{1,0:T(8,128)(2,1)S(1)} collective-permute-done((bf16[64,3072]{1,0:T(8,128)(2,1)S(1)}, bf16[64,3072]{1,0:T(8,128)(2,1)S(1)}, u32[]{:S(2)}, u32[]{:S(2)}) %collective-permute-start.4) | collective-permute-done | bytes 393248 | tf_op jit(solution)/shard_map/while/body/eval_jaxpr/ppermute | solution.py:37
  158.6 10.0 %collective-permute-done.1 = bf16[64,3072]{1,0:T(8,128)(2,1)S(1)} collective-permute-done((bf16[64,3072]{1,0:T(8,128)(2,1)S(1)}, bf16[64,3072]{1,0:T(8,128)(2,1)S(1)}, u32[]{:S(2)}, u32[]{:S(2)}) %collective-permute-start.1) | collective-permute-done | bytes 393248 | tf_op jit(solution)/shard_map/while/body/eval_jaxpr/ppermute | solution.py:37
  168.8 9.3 %collective-permute-start.2 = (bf16[128,3072]{1,0:T(8,128)(2,1)S(1)}, bf16[128,3072]{1,0:T(8,128)(2,1)}, u32[]{:S(2)}, u32[]{:S(2)}) collective-permute-start(bf16[128,3072]{1,0:T(8,128)(2,1)S(1)} %maximum_select_fusion.10), channel_id=1, source_target_pairs={{0,4},{1,5},{2,6},{3,7},{4,0},{5,1},{6,2},{7,3},{8,12},{9,13},{10,... | collective-permute-start | bytes 2359304 | tf_op jit(solution)/shard_map/while/body/eval_jaxpr/ppermute | solution.py:37
  178.8 16.4 %collective-permute-done.2 = bf16[128,3072]{1,0:T(8,128)(2,1)} collective-permute-done((bf16[128,3072]{1,0:T(8,128)(2,1)S(1)}, bf16[128,3072]{1,0:T(8,128)(2,1)}, u32[]{:S(2)}, u32[]{:S(2)}) %collective-permute-start.2) | collective-permute-done | bytes 786464 | tf_op jit(solution)/shard_map/while/body/eval_jaxpr/ppermute | solution.py:37
  197.3 25.0 %conditional.2 = (bf16[1024,768]{0,1:T(8,128)(2,1)}, bf16[128,3072]{1,0:T(8,128)(2,1)S(1)}, bf16[128,3072]{1,0:T(8,128)(2,1)S(1)}) conditional(s32[]{:T(128)} %convert_element_type.288, bf16[1024,768]{0,1:T(8,128)(2,1)} %get-tuple-element.1047, (s32[]{:T(128)}, pred[]{:T(512)}, bf16[256,3072]{1,0:T(8,128)(2,1)S(1)}, bf16[256,3072]{1,0:T(8,128)(2,1)S(1)}, ...), branch_computations={%region_2.2_spmd, %region_3.9_spmd} | conditional | flops 2658447616 | bytes 57946768 | solution.py:228
  224.2 16.4 %collective-permute-done.3 = bf16[128,3072]{1,0:T(8,128)(2,1)S(1)} collective-permute-done((bf16[128,3072]{1,0:T(8,128)(2,1)S(1)}, bf16[128,3072]{1,0:T(8,128)(2,1)S(1)}, u32[]{:S(2)}, u32[]{:S(2)}) %collective-permute-start.3) | collective-permute-done | bytes 786464 | tf_op jit(solution)/shard_map/while/body/eval_jaxpr/ppermute | solution.py:37
  242.2 7.7 %collective-permute-done.4 = bf16[64,3072]{1,0:T(8,128)(2,1)S(1)} collective-permute-done((bf16[64,3072]{1,0:T(8,128)(2,1)S(1)}, bf16[64,3072]{1,0:T(8,128)(2,1)S(1)}, u32[]{:S(2)}, u32[]{:S(2)}) %collective-permute-start.4) | collective-permute-done | bytes 393248 | tf_op jit(solution)/shard_map/while/body/eval_jaxpr/ppermute | solution.py:37
  273.0 10.0 %collective-permute-done.1 = bf16[64,3072]{1,0:T(8,128)(2,1)S(1)} collective-permute-done((bf16[64,3072]{1,0:T(8,128)(2,1)S(1)}, bf16[64,3072]{1,0:T(8,128)(2,1)S(1)}, u32[]{:S(2)}, u32[]{:S(2)}) %collective-permute-start.1) | collective-permute-done | bytes 393248 | tf_op jit(solution)/shard_map/while/body/eval_jaxpr/ppermute | solution.py:37
  283.2 9.6 %collective-permute-start.2 = (bf16[128,3072]{1,0:T(8,128)(2,1)S(1)}, bf16[128,3072]{1,0:T(8,128)(2,1)}, u32[]{:S(2)}, u32[]{:S(2)}) collective-permute-start(bf16[128,3072]{1,0:T(8,128)(2,1)S(1)} %maximum_select_fusion.10), channel_id=1, source_target_pairs={{0,4},{1,5},{2,6},{3,7},{4,0},{5,1},{6,2},{7,3},{8,12},{9,13},{10,... | collective-permute-start | bytes 2359304 | tf_op jit(solution)/shard_map/while/body/eval_jaxpr/ppermute | solution.py:37
  293.5 16.4 %collective-permute-done.2 = bf16[128,3072]{1,0:T(8,128)(2,1)} collective-permute-done((bf16[128,3072]{1,0:T(8,128)(2,1)S(1)}, bf16[128,3072]{1,0:T(8,128)(2,1)}, u32[]{:S(2)}, u32[]{:S(2)}) %collective-permute-start.2) | collective-permute-done | bytes 786464 | tf_op jit(solution)/shard_map/while/body/eval_jaxpr/ppermute | solution.py:37
  312.0 25.0 %conditional.2 = (bf16[1024,768]{0,1:T(8,128)(2,1)}, bf16[128,3072]{1,0:T(8,128)(2,1)S(1)}, bf16[128,3072]{1,0:T(8,128)(2,1)S(1)}) conditional(s32[]{:T(128)} %convert_element_type.288, bf16[1024,768]{0,1:T(8,128)(2,1)} %get-tuple-element.1047, (s32[]{:T(128)}, pred[]{:T(512)}, bf16[256,3072]{1,0:T(8,128)(2,1)S(1)}, bf16[256,3072]{1,0:T(8,128)(2,1)S(1)}, ...), branch_computations={%region_2.2_spmd, %region_3.9_spmd} | conditional | flops 2658447616 | bytes 57946768 | solution.py:228
  338.9 16.4 %collective-permute-done.3 = bf16[128,3072]{1,0:T(8,128)(2,1)S(1)} collective-permute-done((bf16[128,3072]{1,0:T(8,128)(2,1)S(1)}, bf16[128,3072]{1,0:T(8,128)(2,1)S(1)}, u32[]{:S(2)}, u32[]{:S(2)}) %collective-permute-start.3) | collective-permute-done | bytes 786464 | tf_op jit(solution)/shard_map/while/body/eval_jaxpr/ppermute | solution.py:37
  356.9 7.7 %collective-permute-done.4 = bf16[64,3072]{1,0:T(8,128)(2,1)S(1)} collective-permute-done((bf16[64,3072]{1,0:T(8,128)(2,1)S(1)}, bf16[64,3072]{1,0:T(8,128)(2,1)S(1)}, u32[]{:S(2)}, u32[]{:S(2)}) %collective-permute-start.4) | collective-permute-done | bytes 393248 | tf_op jit(solution)/shard_map/while/body/eval_jaxpr/ppermute | solution.py:37
  387.7 10.0 %collective-permute-done.1 = bf16[64,3072]{1,0:T(8,128)(2,1)S(1)} collective-permute-done((bf16[64,3072]{1,0:T(8,128)(2,1)S(1)}, bf16[64,3072]{1,0:T(8,128)(2,1)S(1)}, u32[]{:S(2)}, u32[]{:S(2)}) %collective-permute-start.1) | collective-permute-done | bytes 393248 | tf_op jit(solution)/shard_map/while/body/eval_jaxpr/ppermute | solution.py:37
  397.9 9.6 %collective-permute-start.2 = (bf16[128,3072]{1,0:T(8,128)(2,1)S(1)}, bf16[128,3072]{1,0:T(8,128)(2,1)}, u32[]{:S(2)}, u32[]{:S(2)}) collective-permute-start(bf16[128,3072]{1,0:T(8,128)(2,1)S(1)} %maximum_select_fusion.10), channel_id=1, source_target_pairs={{0,4},{1,5},{2,6},{3,7},{4,0},{5,1},{6,2},{7,3},{8,12},{9,13},{10,... | collective-permute-start | bytes 2359304 | tf_op jit(solution)/shard_map/while/body/eval_jaxpr/ppermute | solution.py:37
  408.2 16.4 %collective-permute-done.2 = bf16[128,3072]{1,0:T(8,128)(2,1)} collective-permute-done((bf16[128,3072]{1,0:T(8,128)(2,1)S(1)}, bf16[128,3072]{1,0:T(8,128)(2,1)}, u32[]{:S(2)}, u32[]{:S(2)}) %collective-permute-start.2) | collective-permute-done | bytes 786464 | tf_op jit(solution)/shard_map/while/body/eval_jaxpr/ppermute | solution.py:37
  426.7 25.0 %conditional.2 = (bf16[1024,768]{0,1:T(8,128)(2,1)}, bf16[128,3072]{1,0:T(8,128)(2,1)S(1)}, bf16[128,3072]{1,0:T(8,128)(2,1)S(1)}) conditional(s32[]{:T(128)} %convert_element_type.288, bf16[1024,768]{0,1:T(8,128)(2,1)} %get-tuple-element.1047, (s32[]{:T(128)}, pred[]{:T(512)}, bf16[256,3072]{1,0:T(8,128)(2,1)S(1)}, bf16[256,3072]{1,0:T(8,128)(2,1)S(1)}, ...), branch_computations={%region_2.2_spmd, %region_3.9_spmd} | conditional | flops 2658447616 | bytes 57946768 | solution.py:228
  453.6 16.4 %collective-permute-done.3 = bf16[128,3072]{1,0:T(8,128)(2,1)S(1)} collective-permute-done((bf16[128,3072]{1,0:T(8,128)(2,1)S(1)}, bf16[128,3072]{1,0:T(8,128)(2,1)S(1)}, u32[]{:S(2)}, u32[]{:S(2)}) %collective-permute-start.3) | collective-permute-done | bytes 786464 | tf_op jit(solution)/shard_map/while/body/eval_jaxpr/ppermute | solution.py:37
  471.7 7.7 %collective-permute-done.4 = bf16[64,3072]{1,0:T(8,128)(2,1)S(1)} collective-permute-done((bf16[64,3072]{1,0:T(8,128)(2,1)S(1)}, bf16[64,3072]{1,0:T(8,128)(2,1)S(1)}, u32[]{:S(2)}, u32[]{:S(2)}) %collective-permute-start.4) | collective-permute-done | bytes 393248 | tf_op jit(solution)/shard_map/while/body/eval_jaxpr/ppermute | solution.py:37
  502.5 10.0 %collective-permute-done.1 = bf16[64,3072]{1,0:T(8,128)(2,1)S(1)} collective-permute-done((bf16[64,3072]{1,0:T(8,128)(2,1)S(1)}, bf16[64,3072]{1,0:T(8,128)(2,1)S(1)}, u32[]{:S(2)}, u32[]{:S(2)}) %collective-permute-start.1) | collective-permute-done | bytes 393248 | tf_op jit(solution)/shard_map/while/body/eval_jaxpr/ppermute | solution.py:37
  512.6 9.6 %collective-permute-start.2 = (bf16[128,3072]{1,0:T(8,128)(2,1)S(1)}, bf16[128,3072]{1,0:T(8,128)(2,1)}, u32[]{:S(2)}, u32[]{:S(2)}) collective-permute-start(bf16[128,3072]{1,0:T(8,128)(2,1)S(1)} %maximum_select_fusion.10), channel_id=1, source_target_pairs={{0,4},{1,5},{2,6},{3,7},{4,0},{5,1},{6,2},{7,3},{8,12},{9,13},{10,... | collective-permute-start | bytes 2359304 | tf_op jit(solution)/shard_map/while/body/eval_jaxpr/ppermute | solution.py:37
  522.9 16.4 %collective-permute-done.2 = bf16[128,3072]{1,0:T(8,128)(2,1)} collective-permute-done((bf16[128,3072]{1,0:T(8,128)(2,1)S(1)}, bf16[128,3072]{1,0:T(8,128)(2,1)}, u32[]{:S(2)}, u32[]{:S(2)}) %collective-permute-start.2) | collective-permute-done | bytes 786464 | tf_op jit(solution)/shard_map/while/body/eval_jaxpr/ppermute | solution.py:37
  543.5 16.4 %collective-permute-done.3 = bf16[128,3072]{1,0:T(8,128)(2,1)S(1)} collective-permute-done((bf16[128,3072]{1,0:T(8,128)(2,1)S(1)}, bf16[128,3072]{1,0:T(8,128)(2,1)S(1)}, u32[]{:S(2)}, u32[]{:S(2)}) %collective-permute-start.3) | collective-permute-done | bytes 786464 | tf_op jit(solution)/shard_map/while/body/eval_jaxpr/ppermute | solution.py:37
  561.5 7.7 %collective-permute-done.4 = bf16[64,3072]{1,0:T(8,128)(2,1)S(1)} collective-permute-done((bf16[64,3072]{1,0:T(8,128)(2,1)S(1)}, bf16[64,3072]{1,0:T(8,128)(2,1)S(1)}, u32[]{:S(2)}, u32[]{:S(2)}) %collective-permute-start.4) | collective-permute-done | bytes 393248 | tf_op jit(solution)/shard_map/while/body/eval_jaxpr/ppermute | solution.py:37
  571.2 30.9 %collective-permute-start.6 = (bf16[32,3072]{1,0:T(8,128)(2,1)S(1)}, bf16[32,3072]{1,0:T(8,128)(2,1)}, u32[]{:S(2)}, u32[]{:S(2)}) collective-permute-start(bf16[32,3072]{1,0:T(8,128)(2,1)S(1)} %get-tuple-element.999), channel_id=1, source_target_pairs={{0,8},{1,9},{2,10},{3,11},{4,12},{5,13},{6,14},{7,15},{16,24},{17,... | collective-permute-start | bytes 589832 | tf_op jit(solution)/shard_map/while/body/eval_jaxpr/ppermute | solution.py:43
  611.9 65.7 %reduce-scatter.2.cloned.1.call-done = f32[48,64]{1,0:T(8,128)} async-done(((f32[768,64]{1,0:T(8,128)}), f32[48,64]{1,0:T(8,128)}) %reduce-scatter.2.cloned.1.call-update) | async-done | bytes 12304 | tf_op jit(solution)/shard_map/reduce_scatter | solution.py:260
  (397 shorter events, 245.5 us)
Async XLA Ops:
  6.5 671.1 %reduce-scatter.2.cloned.1.call-start = ((), (), s32[]{:S(2)}) async-start(), calls=%async_computation.1 | async-start | bytes 417792 | tf_op jit(solution)/shard_map/reduce_scatter | solution.py:260
  18.1 27.7 %collective-permute-start.11 = (bf16[384,64]{1,0:T(8,128)(2,1)S(1)}, bf16[384,64]{1,0:T(8,128)(2,1)S(1)}, u32[]{:S(2)}, u32[]{:S(2)}) collective-permute-start(bf16[384,64]{1,0:T(8,128)(2,1)S(1)} %maximum_select_fusion.4), channel_id=1, source_target_pairs={{0,8},{1,9},{2,10},{3,11},{4,12},{5,13},{6,14},{7,15},{8,0},{9,1},... | collective-permute-start | bytes 147464 | tf_op jit(solution)/shard_map/ppermute | solution.py:28
  54.0 11.4 %collective-permute-start.1 = (bf16[64,3072]{1,0:T(8,128)(2,1)S(1)}, bf16[64,3072]{1,0:T(8,128)(2,1)S(1)}, u32[]{:S(2)}, u32[]{:S(2)}) collective-permute-start(bf16[64,3072]{1,0:T(8,128)(2,1)S(1)} %maximum_select_fusion.9), channel_id=1, source_target_pairs={{0,2},{1,3},{2,0},{3,1},{4,6},{5,7},{6,4},{7,5},{8,10},{9,11},{10,... | collective-permute-start | bytes 1179656 | tf_op jit(solution)/shard_map/while/body/eval_jaxpr/ppermute | solution.py:37
  65.6 19.1 %collective-permute-start.2 = (bf16[128,3072]{1,0:T(8,128)(2,1)S(1)}, bf16[128,3072]{1,0:T(8,128)(2,1)}, u32[]{:S(2)}, u32[]{:S(2)}) collective-permute-start(bf16[128,3072]{1,0:T(8,128)(2,1)S(1)} %maximum_select_fusion.10), channel_id=1, source_target_pairs={{0,4},{1,5},{2,6},{3,7},{4,0},{5,1},{6,2},{7,3},{8,12},{9,13},{10,... | collective-permute-start | bytes 2359304 | tf_op jit(solution)/shard_map/while/body/eval_jaxpr/ppermute | solution.py:37
  111.9 18.1 %collective-permute-start.3 = (bf16[128,3072]{1,0:T(8,128)(2,1)S(1)}, bf16[128,3072]{1,0:T(8,128)(2,1)S(1)}, u32[]{:S(2)}, u32[]{:S(2)}) collective-permute-start(bf16[128,3072]{1,0:T(8,128)(2,1)S(1)} %broadcast_select_fusion.7), channel_id=1, source_target_pairs={{0,4},{1,5},{2,6},{3,7},{4,0},{5,1},{6,2},{7,3},{8,12},{9,13},{10,... | collective-permute-start | bytes 2359304 | tf_op jit(solution)/shard_map/while/body/eval_jaxpr/ppermute | solution.py:37
  130.4 8.9 %collective-permute-start.4 = (bf16[64,3072]{1,0:T(8,128)(2,1)S(1)}, bf16[64,3072]{1,0:T(8,128)(2,1)S(1)}, u32[]{:S(2)}, u32[]{:S(2)}) collective-permute-start(bf16[64,3072]{1,0:T(8,128)(2,1)S(1)} %select_convert_fusion.4), channel_id=1, source_target_pairs={{0,2},{1,3},{2,0},{3,1},{4,6},{5,7},{6,4},{7,5},{8,10},{9,11},{10,... | collective-permute-start | bytes 1179656 | tf_op jit(solution)/shard_map/while/body/eval_jaxpr/ppermute | solution.py:37
  141.3 6.6 collective-permute-start.6
  143.4 8.2 %collective-permute-start.7 = (bf16[32,3072]{1,0:T(8,128)(2,1)S(1)}, bf16[32,3072]{1,0:T(8,128)(2,1)S(1)}, u32[]{:S(2)}, u32[]{:S(2)}) collective-permute-start(bf16[32,3072]{1,0:T(8,128)(2,1)S(1)} %convert_select_fusion.4), channel_id=1, source_target_pairs={{0,8},{1,9},{2,10},{3,11},{4,12},{5,13},{6,14},{7,15},{16,24},{17,... | collective-permute-start | bytes 589832 | tf_op jit(solution)/shard_map/while/body/eval_jaxpr/ppermute | solution.py:43
  157.4 11.2 %collective-permute-start.1 = (bf16[64,3072]{1,0:T(8,128)(2,1)S(1)}, bf16[64,3072]{1,0:T(8,128)(2,1)S(1)}, u32[]{:S(2)}, u32[]{:S(2)}) collective-permute-start(bf16[64,3072]{1,0:T(8,128)(2,1)S(1)} %maximum_select_fusion.9), channel_id=1, source_target_pairs={{0,2},{1,3},{2,0},{3,1},{4,6},{5,7},{6,4},{7,5},{8,10},{9,11},{10,... | collective-permute-start | bytes 1179656 | tf_op jit(solution)/shard_map/while/body/eval_jaxpr/ppermute | solution.py:37
  168.8 26.4 %collective-permute-start.2 = (bf16[128,3072]{1,0:T(8,128)(2,1)S(1)}, bf16[128,3072]{1,0:T(8,128)(2,1)}, u32[]{:S(2)}, u32[]{:S(2)}) collective-permute-start(bf16[128,3072]{1,0:T(8,128)(2,1)S(1)} %maximum_select_fusion.10), channel_id=1, source_target_pairs={{0,4},{1,5},{2,6},{3,7},{4,0},{5,1},{6,2},{7,3},{8,12},{9,13},{10,... | collective-permute-start | bytes 2359304 | tf_op jit(solution)/shard_map/while/body/eval_jaxpr/ppermute | solution.py:37
  222.3 18.2 %collective-permute-start.3 = (bf16[128,3072]{1,0:T(8,128)(2,1)S(1)}, bf16[128,3072]{1,0:T(8,128)(2,1)S(1)}, u32[]{:S(2)}, u32[]{:S(2)}) collective-permute-start(bf16[128,3072]{1,0:T(8,128)(2,1)S(1)} %broadcast_select_fusion.7), channel_id=1, source_target_pairs={{0,4},{1,5},{2,6},{3,7},{4,0},{5,1},{6,2},{7,3},{8,12},{9,13},{10,... | collective-permute-start | bytes 2359304 | tf_op jit(solution)/shard_map/while/body/eval_jaxpr/ppermute | solution.py:37
  241.0 8.9 %collective-permute-start.4 = (bf16[64,3072]{1,0:T(8,128)(2,1)S(1)}, bf16[64,3072]{1,0:T(8,128)(2,1)S(1)}, u32[]{:S(2)}, u32[]{:S(2)}) collective-permute-start(bf16[64,3072]{1,0:T(8,128)(2,1)S(1)} %select_convert_fusion.4), channel_id=1, source_target_pairs={{0,2},{1,3},{2,0},{3,1},{4,6},{5,7},{6,4},{7,5},{8,10},{9,11},{10,... | collective-permute-start | bytes 1179656 | tf_op jit(solution)/shard_map/while/body/eval_jaxpr/ppermute | solution.py:37
  251.9 10.7 %collective-permute-start.6 = (bf16[32,3072]{1,0:T(8,128)(2,1)S(1)}, bf16[32,3072]{1,0:T(8,128)(2,1)}, u32[]{:S(2)}, u32[]{:S(2)}) collective-permute-start(bf16[32,3072]{1,0:T(8,128)(2,1)S(1)} %get-tuple-element.999), channel_id=1, source_target_pairs={{0,8},{1,9},{2,10},{3,11},{4,12},{5,13},{6,14},{7,15},{16,24},{17,... | collective-permute-start | bytes 589832 | tf_op jit(solution)/shard_map/while/body/eval_jaxpr/ppermute | solution.py:43
  258.0 7.9 %collective-permute-start.7 = (bf16[32,3072]{1,0:T(8,128)(2,1)S(1)}, bf16[32,3072]{1,0:T(8,128)(2,1)S(1)}, u32[]{:S(2)}, u32[]{:S(2)}) collective-permute-start(bf16[32,3072]{1,0:T(8,128)(2,1)S(1)} %convert_select_fusion.4), channel_id=1, source_target_pairs={{0,8},{1,9},{2,10},{3,11},{4,12},{5,13},{6,14},{7,15},{16,24},{17,... | collective-permute-start | bytes 589832 | tf_op jit(solution)/shard_map/while/body/eval_jaxpr/ppermute | solution.py:43
  271.8 11.2 %collective-permute-start.1 = (bf16[64,3072]{1,0:T(8,128)(2,1)S(1)}, bf16[64,3072]{1,0:T(8,128)(2,1)S(1)}, u32[]{:S(2)}, u32[]{:S(2)}) collective-permute-start(bf16[64,3072]{1,0:T(8,128)(2,1)S(1)} %maximum_select_fusion.9), channel_id=1, source_target_pairs={{0,2},{1,3},{2,0},{3,1},{4,6},{5,7},{6,4},{7,5},{8,10},{9,11},{10,... | collective-permute-start | bytes 1179656 | tf_op jit(solution)/shard_map/while/body/eval_jaxpr/ppermute | solution.py:37
  283.2 26.7 %collective-permute-start.2 = (bf16[128,3072]{1,0:T(8,128)(2,1)S(1)}, bf16[128,3072]{1,0:T(8,128)(2,1)}, u32[]{:S(2)}, u32[]{:S(2)}) collective-permute-start(bf16[128,3072]{1,0:T(8,128)(2,1)S(1)} %maximum_select_fusion.10), channel_id=1, source_target_pairs={{0,4},{1,5},{2,6},{3,7},{4,0},{5,1},{6,2},{7,3},{8,12},{9,13},{10,... | collective-permute-start | bytes 2359304 | tf_op jit(solution)/shard_map/while/body/eval_jaxpr/ppermute | solution.py:37
  337.1 18.2 %collective-permute-start.3 = (bf16[128,3072]{1,0:T(8,128)(2,1)S(1)}, bf16[128,3072]{1,0:T(8,128)(2,1)S(1)}, u32[]{:S(2)}, u32[]{:S(2)}) collective-permute-start(bf16[128,3072]{1,0:T(8,128)(2,1)S(1)} %broadcast_select_fusion.7), channel_id=1, source_target_pairs={{0,4},{1,5},{2,6},{3,7},{4,0},{5,1},{6,2},{7,3},{8,12},{9,13},{10,... | collective-permute-start | bytes 2359304 | tf_op jit(solution)/shard_map/while/body/eval_jaxpr/ppermute | solution.py:37
  355.7 8.9 %collective-permute-start.4 = (bf16[64,3072]{1,0:T(8,128)(2,1)S(1)}, bf16[64,3072]{1,0:T(8,128)(2,1)S(1)}, u32[]{:S(2)}, u32[]{:S(2)}) collective-permute-start(bf16[64,3072]{1,0:T(8,128)(2,1)S(1)} %select_convert_fusion.4), channel_id=1, source_target_pairs={{0,2},{1,3},{2,0},{3,1},{4,6},{5,7},{6,4},{7,5},{8,10},{9,11},{10,... | collective-permute-start | bytes 1179656 | tf_op jit(solution)/shard_map/while/body/eval_jaxpr/ppermute | solution.py:37
  366.6 10.6 %collective-permute-start.6 = (bf16[32,3072]{1,0:T(8,128)(2,1)S(1)}, bf16[32,3072]{1,0:T(8,128)(2,1)}, u32[]{:S(2)}, u32[]{:S(2)}) collective-permute-start(bf16[32,3072]{1,0:T(8,128)(2,1)S(1)} %get-tuple-element.999), channel_id=1, source_target_pairs={{0,8},{1,9},{2,10},{3,11},{4,12},{5,13},{6,14},{7,15},{16,24},{17,... | collective-permute-start | bytes 589832 | tf_op jit(solution)/shard_map/while/body/eval_jaxpr/ppermute | solution.py:43
  372.7 7.9 %collective-permute-start.7 = (bf16[32,3072]{1,0:T(8,128)(2,1)S(1)}, bf16[32,3072]{1,0:T(8,128)(2,1)S(1)}, u32[]{:S(2)}, u32[]{:S(2)}) collective-permute-start(bf16[32,3072]{1,0:T(8,128)(2,1)S(1)} %convert_select_fusion.4), channel_id=1, source_target_pairs={{0,8},{1,9},{2,10},{3,11},{4,12},{5,13},{6,14},{7,15},{16,24},{17,... | collective-permute-start | bytes 589832 | tf_op jit(solution)/shard_map/while/body/eval_jaxpr/ppermute | solution.py:43
  386.5 11.2 %collective-permute-start.1 = (bf16[64,3072]{1,0:T(8,128)(2,1)S(1)}, bf16[64,3072]{1,0:T(8,128)(2,1)S(1)}, u32[]{:S(2)}, u32[]{:S(2)}) collective-permute-start(bf16[64,3072]{1,0:T(8,128)(2,1)S(1)} %maximum_select_fusion.9), channel_id=1, source_target_pairs={{0,2},{1,3},{2,0},{3,1},{4,6},{5,7},{6,4},{7,5},{8,10},{9,11},{10,... | collective-permute-start | bytes 1179656 | tf_op jit(solution)/shard_map/while/body/eval_jaxpr/ppermute | solution.py:37
  397.9 26.7 %collective-permute-start.2 = (bf16[128,3072]{1,0:T(8,128)(2,1)S(1)}, bf16[128,3072]{1,0:T(8,128)(2,1)}, u32[]{:S(2)}, u32[]{:S(2)}) collective-permute-start(bf16[128,3072]{1,0:T(8,128)(2,1)S(1)} %maximum_select_fusion.10), channel_id=1, source_target_pairs={{0,4},{1,5},{2,6},{3,7},{4,0},{5,1},{6,2},{7,3},{8,12},{9,13},{10,... | collective-permute-start | bytes 2359304 | tf_op jit(solution)/shard_map/while/body/eval_jaxpr/ppermute | solution.py:37
  451.8 18.2 %collective-permute-start.3 = (bf16[128,3072]{1,0:T(8,128)(2,1)S(1)}, bf16[128,3072]{1,0:T(8,128)(2,1)S(1)}, u32[]{:S(2)}, u32[]{:S(2)}) collective-permute-start(bf16[128,3072]{1,0:T(8,128)(2,1)S(1)} %broadcast_select_fusion.7), channel_id=1, source_target_pairs={{0,4},{1,5},{2,6},{3,7},{4,0},{5,1},{6,2},{7,3},{8,12},{9,13},{10,... | collective-permute-start | bytes 2359304 | tf_op jit(solution)/shard_map/while/body/eval_jaxpr/ppermute | solution.py:37
  470.4 8.9 %collective-permute-start.4 = (bf16[64,3072]{1,0:T(8,128)(2,1)S(1)}, bf16[64,3072]{1,0:T(8,128)(2,1)S(1)}, u32[]{:S(2)}, u32[]{:S(2)}) collective-permute-start(bf16[64,3072]{1,0:T(8,128)(2,1)S(1)} %select_convert_fusion.4), channel_id=1, source_target_pairs={{0,2},{1,3},{2,0},{3,1},{4,6},{5,7},{6,4},{7,5},{8,10},{9,11},{10,... | collective-permute-start | bytes 1179656 | tf_op jit(solution)/shard_map/while/body/eval_jaxpr/ppermute | solution.py:37
  481.4 10.6 %collective-permute-start.6 = (bf16[32,3072]{1,0:T(8,128)(2,1)S(1)}, bf16[32,3072]{1,0:T(8,128)(2,1)}, u32[]{:S(2)}, u32[]{:S(2)}) collective-permute-start(bf16[32,3072]{1,0:T(8,128)(2,1)S(1)} %get-tuple-element.999), channel_id=1, source_target_pairs={{0,8},{1,9},{2,10},{3,11},{4,12},{5,13},{6,14},{7,15},{16,24},{17,... | collective-permute-start | bytes 589832 | tf_op jit(solution)/shard_map/while/body/eval_jaxpr/ppermute | solution.py:43
  487.5 7.9 %collective-permute-start.7 = (bf16[32,3072]{1,0:T(8,128)(2,1)S(1)}, bf16[32,3072]{1,0:T(8,128)(2,1)S(1)}, u32[]{:S(2)}, u32[]{:S(2)}) collective-permute-start(bf16[32,3072]{1,0:T(8,128)(2,1)S(1)} %convert_select_fusion.4), channel_id=1, source_target_pairs={{0,8},{1,9},{2,10},{3,11},{4,12},{5,13},{6,14},{7,15},{16,24},{17,... | collective-permute-start | bytes 589832 | tf_op jit(solution)/shard_map/while/body/eval_jaxpr/ppermute | solution.py:43
  501.2 11.2 %collective-permute-start.1 = (bf16[64,3072]{1,0:T(8,128)(2,1)S(1)}, bf16[64,3072]{1,0:T(8,128)(2,1)S(1)}, u32[]{:S(2)}, u32[]{:S(2)}) collective-permute-start(bf16[64,3072]{1,0:T(8,128)(2,1)S(1)} %maximum_select_fusion.9), channel_id=1, source_target_pairs={{0,2},{1,3},{2,0},{3,1},{4,6},{5,7},{6,4},{7,5},{8,10},{9,11},{10,... | collective-permute-start | bytes 1179656 | tf_op jit(solution)/shard_map/while/body/eval_jaxpr/ppermute | solution.py:37
  512.6 26.7 %collective-permute-start.2 = (bf16[128,3072]{1,0:T(8,128)(2,1)S(1)}, bf16[128,3072]{1,0:T(8,128)(2,1)}, u32[]{:S(2)}, u32[]{:S(2)}) collective-permute-start(bf16[128,3072]{1,0:T(8,128)(2,1)S(1)} %maximum_select_fusion.10), channel_id=1, source_target_pairs={{0,4},{1,5},{2,6},{3,7},{4,0},{5,1},{6,2},{7,3},{8,12},{9,13},{10,... | collective-permute-start | bytes 2359304 | tf_op jit(solution)/shard_map/while/body/eval_jaxpr/ppermute | solution.py:37
  541.7 18.2 %collective-permute-start.3 = (bf16[128,3072]{1,0:T(8,128)(2,1)S(1)}, bf16[128,3072]{1,0:T(8,128)(2,1)S(1)}, u32[]{:S(2)}, u32[]{:S(2)}) collective-permute-start(bf16[128,3072]{1,0:T(8,128)(2,1)S(1)} %broadcast_select_fusion.7), channel_id=1, source_target_pairs={{0,4},{1,5},{2,6},{3,7},{4,0},{5,1},{6,2},{7,3},{8,12},{9,13},{10,... | collective-permute-start | bytes 2359304 | tf_op jit(solution)/shard_map/while/body/eval_jaxpr/ppermute | solution.py:37
  560.3 8.9 %collective-permute-start.4 = (bf16[64,3072]{1,0:T(8,128)(2,1)S(1)}, bf16[64,3072]{1,0:T(8,128)(2,1)S(1)}, u32[]{:S(2)}, u32[]{:S(2)}) collective-permute-start(bf16[64,3072]{1,0:T(8,128)(2,1)S(1)} %select_convert_fusion.4), channel_id=1, source_target_pairs={{0,2},{1,3},{2,0},{3,1},{4,6},{5,7},{6,4},{7,5},{8,10},{9,11},{10,... | collective-permute-start | bytes 1179656 | tf_op jit(solution)/shard_map/while/body/eval_jaxpr/ppermute | solution.py:37
  571.2 35.5 %collective-permute-start.6 = (bf16[32,3072]{1,0:T(8,128)(2,1)S(1)}, bf16[32,3072]{1,0:T(8,128)(2,1)}, u32[]{:S(2)}, u32[]{:S(2)}) collective-permute-start(bf16[32,3072]{1,0:T(8,128)(2,1)S(1)} %get-tuple-element.999), channel_id=1, source_target_pairs={{0,8},{1,9},{2,10},{3,11},{4,12},{5,13},{6,14},{7,15},{16,24},{17,... | collective-permute-start | bytes 589832 | tf_op jit(solution)/shard_map/while/body/eval_jaxpr/ppermute | solution.py:43
  602.2 7.9 %collective-permute-start.7 = (bf16[32,3072]{1,0:T(8,128)(2,1)S(1)}, bf16[32,3072]{1,0:T(8,128)(2,1)S(1)}, u32[]{:S(2)}, u32[]{:S(2)}) collective-permute-start(bf16[32,3072]{1,0:T(8,128)(2,1)S(1)} %convert_select_fusion.4), channel_id=1, source_target_pairs={{0,8},{1,9},{2,10},{3,11},{4,12},{5,13},{6,14},{7,15},{16,24},{17,... | collective-permute-start | bytes 589832 | tf_op jit(solution)/shard_map/while/body/eval_jaxpr/ppermute | solution.py:43
  (41 other events, 272.2 us)
Sparse Core Ops, SparseCore 0:
  612.0 65.5 reduce-scatter.1
